TPU v7x, 256 devices: a whole 4x4x8 slice. The times are simulated.
256 devices in a mesh: clip: 4 (over z_hi, core), fsdp: 64 (over y, z_lo, x).
Axes of the slice: x: 4, y: 4, z: 8 (z_hi: 2, z_lo: 4; z = z_hi * 4 + z_lo), core: 2. Of those that a mesh axis runs over, the one named last changes fastest.
Arguments:
- span_queries: bfloat16 [64, 512, 2560], P('fsdp', None, 'clip'), may hold values from -20 to 20
- span_keys: bfloat16 [64, 512, 2560], P('fsdp', None, 'clip'), may hold values from -12 to 12
- span_values: bfloat16 [64, 512, 2560], P('fsdp', None, 'clip'), may hold values from -6 to 6
- cache_keys: bfloat16 [128, 512, 2560], P(None, 'fsdp', 'clip'), may hold values from -6 to 6
- cache_values: bfloat16 [128, 512, 2560], P(None, 'fsdp', 'clip'), may hold values from -6 to 6
- page_table: int32 [128], replicated, may hold values from 0 to 127, each once
- frame_lists: int32 [64, 6], replicated, may hold values from 0 to 15, as said below
- list_counts: int32 [64], replicated, may hold values from 1 to 6, as said below
- out_weight: bfloat16 [2560, 5120], P('clip', 'fsdp'), may hold values from -1 to 1
Outputs:
- projected: bfloat16 [64, 512, 5120], P('fsdp', 'clip')
Inputs may be any that keep to these rules, and one draw needn't show every extreme that they name: `frame_lists`: each row holds 6 different cached frames; a frame attends to the first list_counts of them. `list_counts`: the counts of frames 2 * i and 2 * i + 1 sum to exactly 7; some frame attends to exactly 6. `page_table`: every block number once.
All inputs are finite; a program needn't handle non-finite values.
Results may differ from a plain program's by a relative error of at most 0.017.
Values may be sent and summed in bfloat16 or wider, within the bound.
No kernel may reach another device: no remote copies, remote signals or barrier semaphores. Data moves between devices by JAX's collectives and lax.ppermute only.
A program may use at most 128 MiB of HBM per device.

v0:
```python
import math
import jax
import jax.numpy as jnp
from jax import lax
from jax.sharding import PartitionSpec as P

HD = 128
CF = 8
NC = 16
neg_fill = -1e30


def lookup(values_table, positions):
    table_width = values_table.shape[0]
    matches = positions[..., None] == jnp.arange(table_width, dtype=jnp.int32)
    return jnp.sum(jnp.where(matches, values_table, 0), axis=-1)


def block_numbers(frame_index, slot_index, page_table, frame_lists):
    max_slots = frame_lists.shape[1]
    listed = lookup(frame_lists.reshape(-1), frame_index * max_slots + slot_index)
    return lookup(page_table, frame_index // CF * NC + listed)


def pick_blocks(send_blocks, cache_keys, cache_values):
    slot_total = send_blocks.shape[0]
    frames = send_blocks.shape[1]
    token_slice = cache_keys.shape[1]
    row_width = cache_keys.shape[2]
    sent_keys = cache_keys[send_blocks].reshape(slot_total, frames * token_slice, row_width)
    sent_values = cache_values[send_blocks].reshape(slot_total, frames * token_slice, row_width)
    return (sent_keys, sent_values)


def empty_state(tokens_here, heads_here):
    return (
        jnp.full((tokens_here, heads_here), neg_fill, jnp.float32),
        jnp.zeros((tokens_here, heads_here), jnp.float32),
        jnp.zeros((tokens_here, heads_here, HD), jnp.float32),
    )


def absorb(carried, query_block, key_block, value_block):
    running_max, running_sum, running_out = carried
    scores = jnp.einsum(
        "qhd,khd->qhk", query_block, key_block, preferred_element_type=jnp.float32
    ) * (1.0 / math.sqrt(HD))
    new_max = jnp.maximum(running_max, jnp.max(scores, axis=2))
    shrink = jnp.exp(running_max - new_max)
    weights = jnp.exp(scores - new_max[:, :, None])
    running_sum = running_sum * shrink + jnp.sum(weights, axis=2)
    running_out = running_out * shrink[:, :, None] + jnp.einsum(
        "qhk,khd->qhd",
        weights.astype(jnp.bfloat16),
        value_block,
        preferred_element_type=jnp.float32,
    )
    return (new_max, running_sum, running_out)


def local(
    span_queries,
    span_keys,
    span_values,
    cache_keys,
    cache_values,
    page_table,
    frame_lists,
    list_counts,
    out_weight,
):
    frames = lax.axis_size("fsdp")
    own_frame = lax.axis_index("fsdp")
    tokens_here = span_queries.shape[1]
    row_width = span_queries.shape[2]
    heads_here = row_width // HD
    max_slots = frame_lists.shape[1]
    own_queries = span_queries[0].reshape(tokens_here, heads_here, HD)
    own_keys = span_keys[0].reshape(tokens_here, heads_here, HD)
    own_values = span_values[0].reshape(tokens_here, heads_here, HD)
    destinations = jnp.arange(frames, dtype=jnp.int32)[:, None]
    blank = empty_state(tokens_here, heads_here)
    started = absorb(blank, own_queries, own_keys, own_values)
    slot_index = jnp.arange(max_slots, dtype=jnp.int32)[None, :]
    send_blocks = block_numbers(destinations, slot_index, page_table, frame_lists).T
    sent_keys, sent_values = pick_blocks(send_blocks, cache_keys, cache_values)
    arrived_keys, arrived_values = (
        lax.all_to_all(sent_keys, "fsdp", split_axis=1, concat_axis=1, tiled=True),
        lax.all_to_all(sent_values, "fsdp", split_axis=1, concat_axis=1, tiled=True),
    )
    arrived_keys = arrived_keys.reshape(max_slots, tokens_here, heads_here, HD)
    arrived_values = arrived_values.reshape(max_slots, tokens_here, heads_here, HD)
    item_count = lookup(list_counts, own_frame)

    def advance_own(item_number, carried_one):
        return absorb(
            carried_one, own_queries, arrived_keys[item_number], arrived_values[item_number]
        )

    final_state = lax.fori_loop(0, item_count, advance_own, started)
    running_sum = final_state[1]
    running_out = final_state[2]
    attended = (
        (running_out / running_sum[:, :, None]).astype(jnp.bfloat16).reshape(tokens_here, row_width)
    )
    partial_value = jnp.dot(
        attended,
        lax.all_gather(out_weight, "fsdp", axis=1, tiled=True),
        preferred_element_type=jnp.float32,
    )
    own_rows = lax.psum_scatter(
        partial_value.astype(jnp.bfloat16), "clip", scatter_dimension=0, tiled=True
    )
    return own_rows[None]


def solution(mesh):
    in_specs = (
        P("fsdp", None, "clip"),
        P("fsdp", None, "clip"),
        P("fsdp", None, "clip"),
        P(None, "fsdp", "clip"),
        P(None, "fsdp", "clip"),
        P(),
        P(),
        P(),
        P("clip", "fsdp"),
    )
    out_specs = P("fsdp", "clip", None)
    return jax.shard_map(local, mesh=mesh, in_specs=in_specs, out_specs=out_specs, check_vma=False)
```

profile of v0, /device:TPU:1, one launch (start us, length us, event | category | flops | bytes accessed | tf_op | source)
XLA Modules:
  0.0 632.7 jit_solution(13444650917698095707)
XLA Ops:
  6.5 0.0 copy-start
  6.5 0.9 copy.82
  7.4 0.1 reshape.110
  7.6 0.3 select_reduce_fusion
  7.9 0.9 select_reduce_fusion.1
  8.8 0.1 reshape.118
  8.9 0.0 copy-done
  8.9 3.6 gather_fusion
  12.5 6.8 %copy.83 = bf16[6,512,640]{2,0,1:T(8,128)(2,1)} copy(bf16[6,512,640]{2,1,0:T(8,128)(2,1)} %bitcast.77) | data formatting | bytes 7864320 | tf_op jit(solution)/shard_map/reshape | solution.py:30
  19.3 0.0 copy-start.2
  19.3 12.9 %all-to-all-start = ((bf16[6,512,640]{2,0,1:T(8,128)(2,1)}), bf16[6,512,640]{2,0,1:T(8,128)(2,1)}, u32[]{:S(2)}, u32[]{:S(2)}) async-start(bf16[6,512,640]{2,0,1:T(8,128)(2,1)} %copy.83), calls=%async_computation | async-start | bytes 10485760 | tf_op jit(solution)/shard_map/all_to_all | solution.py:88
  32.2 0.0 copy-done.2
  32.2 3.5 gather_fusion.1
  35.7 6.8 %copy.85 = bf16[6,512,640]{2,0,1:T(8,128)(2,1)} copy(bf16[6,512,640]{2,1,0:T(8,128)(2,1)} %bitcast.76) | data formatting | bytes 7864320 | tf_op jit(solution)/shard_map/reshape | solution.py:31
  42.5 0.0 copy-start.3
  42.5 0.0 copy-start.4
  42.5 0.0 copy-start.5
  42.5 105.9 %all-to-all-done = bf16[6,512,640]{2,0,1:T(8,128)(2,1)} async-done(((bf16[6,512,640]{2,0,1:T(8,128)(2,1)}), bf16[6,512,640]{2,0,1:T(8,128)(2,1)}, u32[]{:S(2)}, u32[]{:S(2)}) %all-to-all-start) | async-done | bytes 3932192 | tf_op jit(solution)/shard_map/all_to_all | solution.py:88
  148.4 8.5 %all-to-all-start.1 = ((bf16[6,512,640]{2,0,1:T(8,128)(2,1)}), bf16[6,512,640]{2,0,1:T(8,128)(2,1)}, u32[]{:S(2)}, u32[]{:S(2)}) async-start(bf16[6,512,640]{2,0,1:T(8,128)(2,1)} %copy.85), calls=%async_computation.1 | async-start | bytes 10485760 | tf_op jit(solution)/shard_map/all_to_all | solution.py:89
  156.9 0.0 all-gather.2.cloned.1.call-start
  156.9 0.7 all-gather.2.cloned.1.call-update
  157.6 0.2 reduce-scatter.2.cloned.1.call-start
  157.9 0.0 copy-done.3
  157.9 0.3 copy.76
  158.1 0.0 copy-done.4
  158.1 0.3 copy.75
  158.4 0.0 copy-done.5
  158.4 0.3 copy.79
  158.7 0.3 copy.89
  159.0 0.9 bitcast_reduce_fusion.1
  159.9 0.9 fusion.23
  160.8 0.0 copy-start.6
  160.8 2.5 fusion.31
  163.4 1.7 copy.87
  165.1 0.0 copy-done.6
  165.1 0.7 fusion.35
  165.8 8.1 %copy.84 = bf16[6,512,640]{1,2,0:T(8,128)(2,1)} copy(bf16[6,512,640]{2,0,1:T(8,128)(2,1)} %all-to-all-done) | data formatting | bytes 7864320 | tf_op jit(solution)/shard_map/all_to_all | solution.py:88
  173.9 119.0 %all-to-all-done.1 = bf16[6,512,640]{2,0,1:T(8,128)(2,1)} async-done(((bf16[6,512,640]{2,0,1:T(8,128)(2,1)}), bf16[6,512,640]{2,0,1:T(8,128)(2,1)}, u32[]{:S(2)}, u32[]{:S(2)}) %all-to-all-start.1) | async-done | bytes 3932192 | tf_op jit(solution)/shard_map/all_to_all | solution.py:89
  292.9 8.1 %copy.86 = bf16[6,512,640]{1,2,0:T(8,128)(2,1)} copy(bf16[6,512,640]{2,0,1:T(8,128)(2,1)} %all-to-all-done.1) | data formatting | bytes 7864320 | tf_op jit(solution)/shard_map/all_to_all | solution.py:89
  301.0 19.1 %while.14 = (s32[]{:T(128)}, f32[512,5]{0,1:T(8,128)S(1)}, f32[512,5]{0,1:T(8,128)S(1)}, f32[512,5,128]{0,2,1:T(8,128)S(1)}, s32[]{:T(128)}, /*index=5*/bf16[6,5...) while((s32[]{:T(128)}, f32[512,5]{0,1:T(8,128)S(1)}, ...), condition=%wide.region_8.9_spmd, body=%wide.region_5.8_spmd.sunk | while | flops 682234880 | bytes 20480152 | solution.py:100
  301.7 2.0 bitcast_reduce_fusion.3
  303.7 0.9 fusion.52
  304.6 2.5 fusion.53
  307.8 2.0 bitcast_reduce_fusion.3
  309.8 0.9 fusion.52
  310.7 2.5 fusion.53
  313.9 2.0 bitcast_reduce_fusion.3
  315.9 0.9 fusion.52
  316.8 2.5 fusion.53
  320.1 0.2 divide_convert_fusion
  320.2 163.1 %all-gather.2.cloned.1.call-done = bf16[640,5120]{0,1:T(8,128)(2,1)} async-done(((bf16[640,80]{0,1:T(8,128)(2,1)}), bf16[640,5120]{0,1:T(8,128)(2,1)}) %all-gather.2.cloned.1.call-update) | async-done | bytes 6553616 | tf_op jit(solution)/shard_map/all_gather | solution.py:108
  483.3 0.0 copy-start.1
  483.3 9.1 %convolution_convert_fusion = bf16[512,5120]{1,0:T(8,128)(2,1)} fusion(bf16[512,640]{0,1:T(8,128)(2,1)S(1)} %bitcast.84, bf16[640,5120]{0,1:T(8,128)(2,1)} %all-gather.2.cloned.1.call-done), kind=kOutput, calls=%fused_computation.22 | convolution fusion | flops 3358064640 | bytes 12451840 | tf_op jit(solution)/shard_map/dot_general | solution.py:106
  492.3 0.0 reduce-scatter.2.cloned.1.call-update
  492.4 133.5 %reduce-scatter.2.cloned.1.call-done = bf16[128,5120]{1,0:T(8,128)(2,1)} async-done(((bf16[512,5120]{1,0:T(8,128)(2,1)}), bf16[128,5120]{1,0:T(8,128)(2,1)}) %reduce-scatter.2.cloned.1.call-update) | async-done | bytes 1310736 | tf_op jit(solution)/shard_map/reduce_scatter | solution.py:111
  625.9 0.0 copy-done.1
  (17 shorter events, 0.1 us)
Async XLA Ops:
  6.5 2.4 copy-start
  19.3 12.9 %copy-start.2 = (bf16[128,8,640]{2,1,0:T(8,128)(2,1)S(1)}, bf16[128,8,640]{2,1,0:T(8,128)(2,1)}, u32[]{:S(2)}) copy-start(bf16[128,8,640]{2,1,0:T(8,128)(2,1)} %param.15) | copy-start | bytes 3932164
  19.3 129.1 %all-to-all-start = ((bf16[6,512,640]{2,0,1:T(8,128)(2,1)}), bf16[6,512,640]{2,0,1:T(8,128)(2,1)}, u32[]{:S(2)}, u32[]{:S(2)}) async-start(bf16[6,512,640]{2,0,1:T(8,128)(2,1)} %copy.83), calls=%async_computation | async-start | bytes 10485760 | tf_op jit(solution)/shard_map/all_to_all | solution.py:88
  42.5 115.4 %copy-start.3 = (bf16[1,512,640]{2,1,0:T(8,128)(2,1)S(1)}, bf16[1,512,640]{2,1,0:T(8,128)(2,1)}, u32[]{:S(2)}) copy-start(bf16[1,512,640]{2,1,0:T(8,128)(2,1)} %param.11) | copy-start | bytes 1966084
  42.5 115.7 %copy-start.4 = (bf16[1,512,640]{2,1,0:T(8,128)(2,1)S(1)}, bf16[1,512,640]{2,1,0:T(8,128)(2,1)}, u32[]{:S(2)}) copy-start(bf16[1,512,640]{2,1,0:T(8,128)(2,1)} %param.12) | copy-start | bytes 1966084
  42.5 115.9 %copy-start.5 = (bf16[1,512,640]{2,1,0:T(8,128)(2,1)S(1)}, bf16[1,512,640]{2,1,0:T(8,128)(2,1)}, u32[]{:S(2)}) copy-start(bf16[1,512,640]{2,1,0:T(8,128)(2,1)} %param.13) | copy-start | bytes 1966084
  148.4 144.5 %all-to-all-start.1 = ((bf16[6,512,640]{2,0,1:T(8,128)(2,1)}), bf16[6,512,640]{2,0,1:T(8,128)(2,1)}, u32[]{:S(2)}, u32[]{:S(2)}) async-start(bf16[6,512,640]{2,0,1:T(8,128)(2,1)} %copy.85), calls=%async_computation.1 | async-start | bytes 10485760 | tf_op jit(solution)/shard_map/all_to_all | solution.py:89
  156.9 326.4 %all-gather.2.cloned.1.call-start = ((), (), s32[]{:S(2)}) async-start(), calls=%async_computation.3 | async-start | bytes 6656000 | tf_op jit(solution)/shard_map/all_gather | solution.py:108
  157.6 468.3 %reduce-scatter.2.cloned.1.call-start = ((), (), s32[]{:S(2)}) async-start(), calls=%async_computation.4 | async-start | bytes 6553600 | tf_op jit(solution)/shard_map/reduce_scatter | solution.py:111
  160.8 4.3 copy-start.6
  483.3 142.6 %copy-start.1 = (bf16[128,8,640]{2,1,0:T(8,128)(2,1)S(1)}, bf16[128,8,640]{2,1,0:T(8,128)(2,1)}, u32[]{:S(2)}) copy-start(bf16[128,8,640]{2,1,0:T(8,128)(2,1)} %param.14) | copy-start | bytes 3932164
Sparse Core Ops, SparseCore 0:
  159.5 323.7 all-gather.1
  492.5 133.3 reduce-scatter.1
where the time goes:
time: 634 us; the launch traced here: 633 us
  waiting for transfers between devices  522 us (82%)
  local copies, waits for them, and re-layouts  40.7 us (6%)
  matrix products  26 us (4%)
  starting transfers between devices  21.6 us (3%)
  between operations  13.6 us (2%)
    all_gather x1, waiting for transfers between devices, local(): lax.all_gather(out_weight, 'fsdp', axis=1, tiled=True)  163 us
    reduce_scatter x1, waiting for transfers between devices, local(): lax.psum_scatter(partial_value.astype(jnp.bfloat16), 'clip', scatter_dime...  134 us
    all_to_all x1, waiting for transfers between devices, local(): lax.all_to_all(sent_values, 'fsdp', split_axis=1, concat_axis=1, tiled=True)  119 us
    all_to_all x1, waiting for transfers between devices, local(): lax.all_to_all(sent_keys, 'fsdp', split_axis=1, concat_axis=1, tiled=True)  106 us
    all_to_all x1, starting transfers between devices, local(): lax.all_to_all(sent_keys, 'fsdp', split_axis=1, concat_axis=1, tiled=True)  12.9 us
  transfers between devices with their start and end apart: 4, of which 4 were waited for; matrix products, arithmetic and copies ran while one was open for 8% of the time, Pallas kernels for 0%

commit v1 on v0

--- a/solution.py
+++ b/solution.py
@@ -105,7 +105,9 @@
     )
     partial_value = jnp.dot(
         attended,
-        lax.all_gather(out_weight, "fsdp", axis=1, tiled=True),
+        jnp.concatenate(
+            lax.all_to_all(jnp.stack([out_weight] * lax.axis_size("fsdp")), "fsdp", 0, 0), axis=1
+        ),
         preferred_element_type=jnp.float32,
     )
     own_rows = lax.psum_scatter(

time: 634 us -> 542 us (0.85)
  waiting for transfers between devices: 522 us -> 303 us
  blocking collectives: 0 us -> 127 us
    all_gather x1 -> x0, waiting for transfers between devices: 163 us -> none  [local(): lax.all_gather(out_weight, 'fsdp', axis=1, tiled=True)]
    all_to_all x0 -> x1, blocking collectives: none -> 127 us  [local(): lax.all_to_all(sent_values, 'fsdp', split_axis=1, concat_axis=1, tiled=True)]
    reduce_scatter x1, waiting for transfers between devices: 134 us -> 97 us  [local(): lax.psum_scatter(partial_value.astype(jnp.bfloat16), 'clip', scatter_dime...]
    all_to_all x1, waiting for transfers between devices: 119 us -> 100 us  [local(): lax.all_to_all(jnp.stack([out_weight] * lax.axis_size('fsdp')), 'fsdp', 0...]
  transfers between devices with their start and end apart: 4 -> 3, of which waited for: 4 -> 3; matrix products, arithmetic and copies ran while one was open for 8% -> 9% of each run, Pallas kernels for 0% -> 0%
where the time goes in v1:
time: 542 us; the launch traced here: 541 us
  waiting for transfers between devices  303 us (56%)
  blocking collectives  127 us (23%)
  local copies, waits for them, and re-layouts  44.1 us (8%)
  matrix products  26 us (5%)
  starting transfers between devices  19.2 us (4%)
  between operations  13.6 us (3%)
  other arithmetic  5.64 us (1%)
    all_to_all x1, blocking collectives, local(): lax.all_to_all(sent_values, 'fsdp', split_axis=1, concat_axis=1, tiled=True)  127 us
    all_to_all x1, waiting for transfers between devices, local(): lax.all_to_all(sent_keys, 'fsdp', split_axis=1, concat_axis=1, tiled=True)  106 us
    all_to_all x1, waiting for transfers between devices, local(): lax.all_to_all(jnp.stack([out_weight] * lax.axis_size('fsdp')), 'fsdp', 0...  100 us
    reduce_scatter x1, waiting for transfers between devices, local(): lax.psum_scatter(partial_value.astype(jnp.bfloat16), 'clip', scatter_dime...  97 us
    all_to_all x1, starting transfers between devices, local(): lax.all_to_all(sent_keys, 'fsdp', split_axis=1, concat_axis=1, tiled=True)  12.9 us
  transfers between devices with their start and end apart: 3, of which 3 were waited for; matrix products, arithmetic and copies ran while one was open for 9% of the time, Pallas kernels for 0%

profile of v1, /device:TPU:1, one launch (start us, length us, event | category | flops | bytes accessed | tf_op | source)
XLA Modules:
  0.0 540.7 jit_solution(5276696983144412220)
XLA Ops:
  6.5 0.0 copy-start
  6.5 0.9 copy.83
  7.4 0.1 reshape.118
  7.6 0.3 select_reduce_fusion
  7.9 0.9 select_reduce_fusion.1
  8.8 0.1 reshape.128
  8.9 0.0 copy-done
  8.9 3.6 gather_fusion
  12.5 6.8 %copy.84 = bf16[6,512,640]{2,0,1:T(8,128)(2,1)} copy(bf16[6,512,640]{2,1,0:T(8,128)(2,1)} %bitcast.80) | data formatting | bytes 7864320 | tf_op jit(solution)/shard_map/reshape | solution.py:30
  19.3 0.0 copy-start.2
  19.3 12.9 %all-to-all-start = ((bf16[6,512,640]{2,0,1:T(8,128)(2,1)}), bf16[6,512,640]{2,0,1:T(8,128)(2,1)}, u32[]{:S(2)}, u32[]{:S(2)}) async-start(bf16[6,512,640]{2,0,1:T(8,128)(2,1)} %copy.84), calls=%async_computation | async-start | bytes 10485760 | tf_op jit(solution)/shard_map/all_to_all | solution.py:88
  32.2 0.0 copy-done.2
  32.2 3.5 gather_fusion.1
  35.7 6.8 %copy.86 = bf16[6,512,640]{2,0,1:T(8,128)(2,1)} copy(bf16[6,512,640]{2,1,0:T(8,128)(2,1)} %bitcast.79) | data formatting | bytes 7864320 | tf_op jit(solution)/shard_map/reshape | solution.py:31
  42.6 0.0 copy-start.6
  42.6 105.8 %all-to-all-done = bf16[6,512,640]{2,0,1:T(8,128)(2,1)} async-done(((bf16[6,512,640]{2,0,1:T(8,128)(2,1)}), bf16[6,512,640]{2,0,1:T(8,128)(2,1)}, u32[]{:S(2)}, u32[]{:S(2)}) %all-to-all-start) | async-done | bytes 3932192 | tf_op jit(solution)/shard_map/all_to_all | solution.py:88
  148.4 126.5 %all_to_all.15 = bf16[6,512,640]{2,0,1:T(8,128)(2,1)} all-to-all(bf16[6,512,640]{2,0,1:T(8,128)(2,1)} %copy.86), channel_id=1, replica_groups=mesh['clip'=4,'fsdp'=64] {'fsdp'}, dimensions={1} | all-to-all | bytes 7864320 | tf_op jit(solution)/shard_map/all_to_all | solution.py:89
  274.9 0.0 copy-done.6
  274.9 3.2 stack.2
  278.1 0.0 copy-start.3
  278.1 0.0 copy-start.4
  278.1 0.0 copy-start.5
  278.1 6.0 %all-to-all-start.2 = ((bf16[64,640,80]{1,2,0:T(8,128)(2,1)}), bf16[64,640,80]{1,2,0:T(8,128)(2,1)}, u32[]{:S(2)}, u32[]{:S(2)}) async-start(bf16[64,640,80]{1,2,0:T(8,128)(2,1)} %stack.2), calls=%async_computation.2 | async-start | bytes 13107200 | tf_op jit(solution)/shard_map/all_to_all | solution.py:109
  284.2 0.2 reduce-scatter.2.cloned.1.call-start
  284.4 0.0 copy-done.3
  284.4 0.3 copy.77
  284.7 0.0 copy-done.4
  284.7 0.3 copy.76
  285.0 0.0 copy-done.5
  285.0 0.3 copy.80
  285.2 0.3 copy.90
  285.6 0.9 bitcast_reduce_fusion.1
  286.5 0.9 fusion.23
  287.4 0.0 copy-start.7
  287.4 2.5 fusion.31
  289.9 1.7 copy.88
  291.7 0.0 copy-done.7
  291.7 0.7 fusion.35
  292.4 8.1 %copy.85 = bf16[6,512,640]{1,2,0:T(8,128)(2,1)} copy(bf16[6,512,640]{2,0,1:T(8,128)(2,1)} %all-to-all-done) | data formatting | bytes 7864320 | tf_op jit(solution)/shard_map/all_to_all | solution.py:88
  300.4 8.1 %copy.87 = bf16[6,512,640]{1,2,0:T(8,128)(2,1)} copy(bf16[6,512,640]{2,0,1:T(8,128)(2,1)} %all_to_all.15) | data formatting | bytes 7864320 | tf_op jit(solution)/shard_map/all_to_all | solution.py:89
  308.6 19.0 %while.14 = (s32[]{:T(128)}, f32[512,5]{0,1:T(8,128)S(1)}, f32[512,5]{0,1:T(8,128)S(1)}, f32[512,5,128]{0,2,1:T(8,128)S(1)}, s32[]{:T(128)}, /*index=5*/bf16[6,5...) while((s32[]{:T(128)}, f32[512,5]{0,1:T(8,128)S(1)}, ...), condition=%wide.region_8.9_spmd, body=%wide.region_5.8_spmd.sunk | while | flops 682234880 | bytes 20480152 | solution.py:100
  309.3 2.0 bitcast_reduce_fusion.3
  311.3 0.9 fusion.52
  312.2 2.5 fusion.53
  315.4 2.0 bitcast_reduce_fusion.3
  317.4 0.9 fusion.52
  318.3 2.5 fusion.53
  321.5 2.0 bitcast_reduce_fusion.3
  323.5 0.9 fusion.52
  324.4 2.5 fusion.53
  327.6 0.2 divide_convert_fusion
  327.8 100.0 %all-to-all-done.2 = bf16[64,640,80]{1,2,0:T(8,128)(2,1)} async-done(((bf16[64,640,80]{1,2,0:T(8,128)(2,1)}), bf16[64,640,80]{1,2,0:T(8,128)(2,1)}, u32[]{:S(2)}, u32[]{:S(2)}) %all-to-all-start.2) | async-done | bytes 6553632 | tf_op jit(solution)/shard_map/all_to_all | solution.py:109
  427.8 0.0 copy-start.1
  427.8 9.1 %convolution_convert_fusion = bf16[512,5120]{1,0:T(8,128)(2,1)} fusion(bf16[512,640]{0,1:T(8,128)(2,1)S(1)} %bitcast.87, bf16[640,5120]{0,1:T(8,128)(2,1)} %bitcast.16), kind=kOutput, calls=%fused_computation.22 | convolution fusion | flops 3358064640 | bytes 12451840 | tf_op jit(solution)/shard_map/dot_general | solution.py:106
  436.8 0.0 reduce-scatter.2.cloned.1.call-update
  436.9 97.0 %reduce-scatter.2.cloned.1.call-done = bf16[128,5120]{1,0:T(8,128)(2,1)} async-done(((bf16[512,5120]{1,0:T(8,128)(2,1)}), bf16[128,5120]{1,0:T(8,128)(2,1)}) %reduce-scatter.2.cloned.1.call-update) | async-done | bytes 1310736 | tf_op jit(solution)/shard_map/reduce_scatter | solution.py:113
  533.9 0.0 copy-done.1
  (17 shorter events, 0.1 us)
Async XLA Ops:
  6.5 2.4 copy-start
  19.3 12.9 %copy-start.2 = (bf16[128,8,640]{2,1,0:T(8,128)(2,1)S(1)}, bf16[128,8,640]{2,1,0:T(8,128)(2,1)}, u32[]{:S(2)}) copy-start(bf16[128,8,640]{2,1,0:T(8,128)(2,1)} %param.15) | copy-start | bytes 3932164
  19.3 129.1 %all-to-all-start = ((bf16[6,512,640]{2,0,1:T(8,128)(2,1)}), bf16[6,512,640]{2,0,1:T(8,128)(2,1)}, u32[]{:S(2)}, u32[]{:S(2)}) async-start(bf16[6,512,640]{2,0,1:T(8,128)(2,1)} %copy.84), calls=%async_computation | async-start | bytes 10485760 | tf_op jit(solution)/shard_map/all_to_all | solution.py:88
  42.6 232.3 %copy-start.6 = (bf16[640,80]{0,1:T(8,128)(2,1)S(1)}, bf16[640,80]{0,1:T(8,128)(2,1)}, u32[]{:S(2)}) copy-start(bf16[640,80]{0,1:T(8,128)(2,1)} %param.19) | copy-start | bytes 307204
  278.1 6.3 %copy-start.3 = (bf16[1,512,640]{2,1,0:T(8,128)(2,1)S(1)}, bf16[1,512,640]{2,1,0:T(8,128)(2,1)}, u32[]{:S(2)}) copy-start(bf16[1,512,640]{2,1,0:T(8,128)(2,1)} %param.11) | copy-start | bytes 1966084
  278.1 6.6 %copy-start.4 = (bf16[1,512,640]{2,1,0:T(8,128)(2,1)S(1)}, bf16[1,512,640]{2,1,0:T(8,128)(2,1)}, u32[]{:S(2)}) copy-start(bf16[1,512,640]{2,1,0:T(8,128)(2,1)} %param.12) | copy-start | bytes 1966084
  278.1 6.8 %copy-start.5 = (bf16[1,512,640]{2,1,0:T(8,128)(2,1)S(1)}, bf16[1,512,640]{2,1,0:T(8,128)(2,1)}, u32[]{:S(2)}) copy-start(bf16[1,512,640]{2,1,0:T(8,128)(2,1)} %param.13) | copy-start | bytes 1966084
  278.1 149.6 %all-to-all-start.2 = ((bf16[64,640,80]{1,2,0:T(8,128)(2,1)}), bf16[64,640,80]{1,2,0:T(8,128)(2,1)}, u32[]{:S(2)}, u32[]{:S(2)}) async-start(bf16[64,640,80]{1,2,0:T(8,128)(2,1)} %stack.2), calls=%async_computation.2 | async-start | bytes 13107200 | tf_op jit(solution)/shard_map/all_to_all | solution.py:109
  284.2 249.7 %reduce-scatter.2.cloned.1.call-start = ((), (), s32[]{:S(2)}) async-start(), calls=%async_computation.4 | async-start | bytes 6553600 | tf_op jit(solution)/shard_map/reduce_scatter | solution.py:113
  287.4 4.3 copy-start.7
  427.8 106.1 %copy-start.1 = (bf16[128,8,640]{2,1,0:T(8,128)(2,1)S(1)}, bf16[128,8,640]{2,1,0:T(8,128)(2,1)}, u32[]{:S(2)}) copy-start(bf16[128,8,640]{2,1,0:T(8,128)(2,1)} %param.14) | copy-start | bytes 3932164
Sparse Core Ops, SparseCore 0:
  437.0 96.8 reduce-scatter.1
